TPU v7x, 256 devices: a whole 4x4x8 slice. The times are simulated.
256 devices in a mesh: wall: 8 (over y_lo, x), stream: 32 (over z, y_hi, core).
Axes of the slice: x: 4, y: 4 (y_hi: 2, y_lo: 2; y = y_hi * 2 + y_lo), z: 8, core: 2. Of those that a mesh axis runs over, the one named last changes fastest.
Arguments:
- velocity: float32 [3, 64, 512, 128], P(None, 'wall', 'stream'), may hold values from -6 to 6
- sample_block: int32 [8, 256], P('wall', 'stream'), may hold values from 0 to 127
- sample_member: int32 [8, 256, 1], P('wall', 'stream'), may hold values from 0 to 7; in each aligned block of 8 rows (0 to 7, 8 to 15, ..., all dimensions but the last counted through in order) at most 2 rows name the same one
- k_first: bfloat16 [8, 54, 64], P('wall'), may hold values from -6 to 6
- k_second: bfloat16 [8, 27, 64, 64], P('wall'), may hold values from -6 to 6
- w_hidden: bfloat16 [8, 2048, 2048], P('wall'), may hold values from -6 to 6
- w_out: bfloat16 [8, 2048, 2], P('wall'), may hold values from -6 to 6
Outputs:
- new_field: float32 [3, 64, 512, 128], P(None, 'wall', 'stream')
- stress: float32 [2, 8, 256], P(None, 'wall', 'stream')
- new_k_first: float32 [8, 54, 64], P('wall')
- new_k_second: float32 [8, 27, 64, 64], P('wall')
- new_w_hidden: float32 [8, 2048, 2048], P('wall', 'stream')
- new_w_out: float32 [8, 2048, 2], P('wall')
Inputs may be any that keep to these rules, and one draw needn't show every extreme that they name: `sample_member`: in the list of one slab at most 2 samples name the same member; in every draw some slab names some member exactly 2 times.
All inputs are finite; a program needn't handle non-finite values.
Results may differ from a plain program's by a relative error of at most 0.0064.
Values may be sent and summed in bfloat16 or wider, within the bound.
No kernel may reach another device: no remote copies, remote signals or barrier semaphores. Data moves between devices by JAX's collectives and lax.ppermute only.
A program may use at most 128 MiB of HBM per device.

v0:
```python
import math
import jax
import jax.numpy as jnp
import numpy as np
from jax import lax
from jax.sharding import Mesh
from jax.sharding import PartitionSpec as P

P_SIZE = 8
PY = 4
PX = 4
PZ = 8
CH = 64
CAP = 2
FEATS = 2048
STREAM = ("stream_0", "stream_1", "stream_2")
highest = lax.Precision.HIGHEST
time_step = 0.005
relax_rate = 20.0
viscosity = 0.3
learn_rate = 0.5
rms_eps = 1e-06


def extended(shard, sides, width):
    edges = {}
    for axis, dim in sides:
        size, length = (lax.axis_size(axis), shard.shape[dim])
        up = [(i, (i + 1) % size) for i in range(size)]
        last = lax.slice_in_dim(shard, length - width, length, axis=dim)
        first = lax.slice_in_dim(shard, 0, width, axis=dim)
        edges[dim] = (
            lax.ppermute(last, axis, up),
            lax.ppermute(first, axis, [(b, a) for a, b in up]),
        )
    done = []
    for _, dim in sides:
        low, high = edges[dim]
        around = [(width, width) if d in done else (0, 0) for d in range(shard.ndim)]
        shard = jnp.concatenate([jnp.pad(low, around), shard, jnp.pad(high, around)], axis=dim)
        done.append(dim)
    return shard


def in_one_piece(arrays, axis, split_dim, concat_dim, along):
    widths = [math.prod(a.shape[along:]) for a in arrays]
    both = jnp.concatenate(
        [a.reshape(*a.shape[:along], w) for a, w in zip(arrays, widths)], axis=along
    )
    whole = lax.all_to_all(both, axis, split_axis=split_dim, concat_axis=concat_dim, tiled=True)
    tiles = jnp.split(whole, [sum(widths[:k]) for k in range(1, len(widths))], axis=along)
    return tuple((b.reshape(*whole.shape[:along], *a.shape[along:]) for a, b in zip(arrays, tiles)))


def joined_along(tiles, dim):
    lengths = list(tiles.shape[1:])
    lengths[dim] *= tiles.shape[0]
    return jnp.moveaxis(tiles, 0, dim).reshape(lengths)


def gather_in_order(shard, axes, order):
    tiles = shard
    for k in order:
        tiles = lax.all_gather(tiles, axes[k])
    done = order[::-1]
    back = [done.index(k) for k in range(len(axes))]
    tiles = tiles.transpose(*back, *range(len(axes), tiles.ndim))
    return tiles.reshape(-1, *shard.shape)


def gathered_by_axis(shard, axes, order, dim):
    return joined_along(gather_in_order(shard, axes, order), dim)


def cheb_tables(points):
    order = points - 1
    node_index = np.arange(points)
    nodes = -np.cos(np.pi * node_index / order)
    end_weight = np.where((node_index == 0) | (node_index == order), 2.0, 1.0)
    parity = (-1.0) ** (node_index[:, None] + node_index[None, :])
    offdiag = 1.0 - np.eye(points)
    spread = nodes[:, None] - nodes[None, :] + np.eye(points)
    deriv = end_weight[:, None] / end_weight[None, :] * parity / spread * offdiag
    deriv = deriv - np.eye(points) * deriv.sum(axis=1)[:, None]
    highpass = parity / (order * end_weight[None, :])
    return (deriv, highpass, 0.5 * order * order)


def axis_matrices(count, periodic):
    deriv, highpass, lift_half = cheb_tables(P_SIZE)
    length = count * P_SIZE
    slope = np.kron(np.eye(count), deriv)
    upper = np.kron(np.eye(count), highpass)
    faces = count if periodic else count - 1
    for element in range(faces):
        last_node = element * P_SIZE + P_SIZE - 1
        next_node = (element + 1) % count * P_SIZE
        slope[last_node, next_node] += lift_half
        slope[last_node, last_node] -= lift_half
        slope[next_node, last_node] -= lift_half
        slope[next_node, next_node] += lift_half
    if not periodic:
        slope[0, 0] += lift_half
        slope[length - 1, length - 1] -= lift_half
    paired = jnp.asarray(np.concatenate([slope, upper], axis=0), jnp.float32)
    return (paired, lift_half)


def slot_matrix(members, member_count):
    member_hot = (members[..., None] == jnp.arange(member_count, dtype=jnp.int32)).astype(jnp.int32)
    before = jnp.cumsum(member_hot, axis=-2) - member_hot
    ranks = jnp.sum(before * member_hot, axis=-1)
    slots = members * CAP + ranks
    return (slots[..., None, :] == jnp.arange(member_count * CAP, dtype=jnp.int32)[:, None]).astype(
        jnp.float32
    )


DIMS = ("NDHWC", "DHWIO", "NDHWC")
FILTER_DIMS = ("CDHWN", "IDHWO", "NDHWC")
SAME = ((1, 1), (1, 1), (1, 1))


def silu_slope(value):
    gate = jax.nn.sigmoid(value)
    return gate * (1.0 + value * (1.0 - gate))


def conv_taps(grid, kernel):
    return lax.conv_general_dilated(
        grid, kernel, (1, 1, 1), SAME, dimension_numbers=DIMS, preferred_element_type=jnp.float32
    )


def conv_filter(grid, delta):
    taps = lax.conv_general_dilated(
        grid,
        delta,
        (1, 1, 1),
        SAME,
        dimension_numbers=FILTER_DIMS,
        preferred_element_type=jnp.float32,
    )
    return jnp.moveaxis(taps, 0, 3)


def forward_back(patches, aim_rows, valid, k_first, k_second, w_hidden, w_out):
    batch = patches.shape[0]
    channels = k_second.shape[-1]
    inputs = patches.reshape(batch, 2, PY, PX, PZ).transpose(0, 2, 3, 4, 1)
    first_taps = k_first.reshape(3, 3, 3, 2, channels)
    second_taps = k_second.reshape(3, 3, 3, channels, channels)
    scale_one = 1.0 / math.sqrt(54.0)
    scale_two = 1.0 / math.sqrt(27.0 * channels)
    scale_three = 1.0 / math.sqrt(1.0 * w_hidden.shape[0])
    scale_four = 1.0 / math.sqrt(1.0 * w_hidden.shape[1])
    pre_one = conv_taps(inputs, first_taps) * scale_one
    hidden_one = jax.nn.silu(pre_one).astype(jnp.bfloat16)
    pre_two = conv_taps(hidden_one, second_taps) * scale_two
    pooled = (
        jax.nn.silu(pre_two).reshape(batch, PY // 2, 2, PX // 2, 2, PZ, channels).mean(axis=(2, 4))
    )
    features = pooled.reshape(batch, -1).astype(jnp.bfloat16)
    pre_three = jnp.dot(features, w_hidden, preferred_element_type=jnp.float32) * scale_three
    hidden_three = jax.nn.silu(pre_three).astype(jnp.bfloat16)
    pred = jnp.dot(hidden_three, w_out, preferred_element_type=jnp.float32) * scale_four
    error = valid.astype(jnp.float32)[:, None] * (pred - aim_rows.astype(jnp.float32))
    grad_out = jnp.dot(hidden_three.astype(jnp.float32).T, error, precision=highest) * scale_four
    delta_three = (
        jnp.dot(error, w_out.astype(jnp.float32).T, precision=highest)
        * scale_four
        * silu_slope(pre_three)
    ).astype(jnp.bfloat16)
    back_feat = jnp.dot(delta_three, w_hidden.T, preferred_element_type=jnp.float32) * scale_three
    back_grid = back_feat.reshape(batch, PY // 2, 1, PX // 2, 1, PZ, channels)
    spread_back = (
        jnp.broadcast_to(back_grid, (batch, PY // 2, 2, PX // 2, 2, PZ, channels)).reshape(
            pre_two.shape
        )
        * 0.25
    )
    delta_two = (spread_back * silu_slope(pre_two)).astype(jnp.bfloat16)
    grad_two = (conv_filter(hidden_one, delta_two) * scale_two).reshape(27, channels, channels)
    mirrored = jnp.flip(second_taps, axis=(0, 1, 2)).swapaxes(3, 4)
    back_one = conv_taps(delta_two, mirrored)
    delta_one = (back_one * scale_two * silu_slope(pre_one)).astype(jnp.bfloat16)
    grad_one = (conv_filter(inputs, delta_one) * scale_one).reshape(54, channels)
    return (pred, grad_one, grad_two, grad_out, features, delta_three)


def row_update(weight, grad):
    scale = jnp.sqrt(jnp.mean(grad * grad, axis=-1, keepdims=True) + rms_eps)
    return weight.astype(jnp.float32) - learn_rate * grad / scale


def whole_update(weight, grad):
    scale = jnp.sqrt(jnp.mean(grad * grad) + rms_eps)
    return weight.astype(jnp.float32) - learn_rate * grad / scale


def body(velocity, sample_block, sample_member, k_first, k_second, w_hidden, w_out):
    wall_count = lax.axis_size("wall")
    wall_place = lax.axis_index("wall")
    flow_count = lax.axis_size(STREAM)
    flow_place = lax.axis_index(STREAM)
    padded = extended(velocity, (("wall", 1), (STREAM, 2)), 1)
    keep_low = (wall_place > 0).astype(jnp.float32)
    keep_high = (wall_place < wall_count - 1).astype(jnp.float32)
    below = padded[:, 0, 1:-1, :] * keep_low
    above = padded[:, -1, 1:-1, :] * keep_high
    left_face = padded[:, 1:-1, 0, :]
    right_face = padded[:, 1:-1, -1, :]
    size_y, size_x, size_z = (velocity.shape[1], velocity.shape[2], velocity.shape[3])
    pair_y, lift_half = axis_matrices(size_y // P_SIZE, False)
    pair_x, lift_same = axis_matrices(size_x // P_SIZE, False)
    pair_z, lift_again = axis_matrices(size_z // P_SIZE, True)
    along_y = jnp.einsum("cyxz,wy->cwxz", velocity, pair_y, precision=highest)
    grad_y = (
        along_y[:, :size_y]
        .at[:, 0]
        .add(-lift_half * below)
        .at[:, size_y - 1]
        .add(lift_half * above)
    )
    high_y = along_y[:, size_y:]
    along_x = jnp.einsum("cyxz,wx->cywz", velocity, pair_x, precision=highest)
    grad_x = (
        along_x[:, :, :size_x]
        .at[:, :, 0]
        .add(-lift_half * left_face)
        .at[:, :, size_x - 1]
        .add(lift_half * right_face)
    )
    high_x = along_x[:, :, size_x:]
    along_z = jnp.einsum("cyxz,wz->cyxw", velocity, pair_z, precision=highest)
    grad_z = along_z[..., :size_z]
    high_z = along_z[..., size_z:]
    advect = velocity[0][None] * grad_x + velocity[1][None] * grad_y + velocity[2][None] * grad_z
    new_field = velocity + time_step * (-advect - relax_rate * (high_x + high_y + high_z))
    rows_y, rows_x, rows_z = (size_y // PY, size_x // PX, size_z // PZ)
    tangent = jnp.stack([velocity[0], velocity[2]]).reshape(2, rows_y, PY, rows_x, PX, rows_z, PZ)
    blocks = tangent.transpose(1, 3, 5, 0, 2, 4, 6).reshape(-1, 2 * PY * PX * PZ)
    slope_wall = jnp.stack([grad_y[0], grad_y[2]]).reshape(2, rows_y, PY, rows_x, PX, rows_z, PZ)
    stress_true = (
        (viscosity * jnp.mean(slope_wall, axis=(2, 4, 6))).transpose(1, 2, 3, 0).reshape(-1, 2)
    )
    picked = sample_block.reshape(-1)
    members = sample_member.reshape(-1)
    patch_rows = jnp.take(blocks, picked, axis=0).astype(jnp.bfloat16)
    aim_rows = jnp.take(stress_true, picked, axis=0).astype(jnp.bfloat16)
    select = slot_matrix(members, wall_count)
    select_half = select.astype(jnp.bfloat16)
    send_rows = jnp.dot(select_half, patch_rows, preferred_element_type=jnp.float32).astype(
        jnp.bfloat16
    )
    send_aims = jnp.dot(select_half, aim_rows, preferred_element_type=jnp.float32).astype(
        jnp.bfloat16
    )
    send_valid = jnp.sum(select, axis=1).astype(jnp.bfloat16)
    recv_rows, recv_aims, recv_valid = in_one_piece(
        (send_rows, send_aims, send_valid), "wall", 0, 0, 1
    )
    pred, grad_one, grad_two, grad_out, features, delta_three = forward_back(
        recv_rows, recv_aims, recv_valid, k_first[0], k_second[0], w_hidden[0], w_out[0]
    )
    back = lax.all_to_all(pred, "wall", split_axis=0, concat_axis=0, tiled=True)
    stress_local = jnp.dot(select.T, back, precision=highest)
    stress = stress_local.T[:, None, :]
    share_rows = FEATS // flow_count
    dense_scale = 1.0 / math.sqrt(1.0 * FEATS)
    columns_here = lax.all_to_all(features, STREAM, split_axis=1, concat_axis=0, tiled=True)
    grad_hidden = (
        jnp.dot(
            columns_here.T,
            gathered_by_axis(delta_three, STREAM, (1, 0, 2), 0),
            preferred_element_type=jnp.float32,
        )
        * dense_scale
    )
    own_rows = lax.dynamic_slice_in_dim(w_hidden[0], flow_place * share_rows, share_rows, 0)
    new_w_hidden = row_update(own_rows, grad_hidden)[None]
    grad_one, grad_two, grad_out = lax.psum((grad_one, grad_two, grad_out), STREAM)
    new_k_second = row_update(k_second[0], grad_two)
    new_k_first = row_update(k_first[0], grad_one)
    new_w_out = whole_update(w_out[0], grad_out)
    return (new_field, stress, new_k_first[None], new_k_second[None], new_w_hidden, new_w_out[None])


def solution(mesh):
    torus = Mesh(
        mesh.devices.reshape(mesh.shape["wall"], 8, 2, 2),
        ("wall", "stream_0", "stream_1", "stream_2"),
    )
    in_specs = (
        P(None, "wall", STREAM, None),
        P("wall", STREAM),
        P("wall", STREAM, None),
        P("wall", None, None),
        P("wall", None, None, None),
        P("wall", None, None),
        P("wall", None, None),
    )
    out_specs = (
        P(None, "wall", STREAM, None),
        P(None, "wall", STREAM),
        P("wall", None, None),
        P("wall", None, None, None),
        P("wall", STREAM, None),
        P("wall", None, None),
    )
    return jax.shard_map(body, mesh=torus, in_specs=in_specs, out_specs=out_specs, check_vma=False)
```

profile of v0, /device:TPU:1, one launch (start us, length us, event | category | flops | bytes accessed | tf_op | source)
XLA Modules:
  0.0 358.8 jit_solution(1956748719228689826)
XLA Ops:
  8.8 2.0 collective-permute-start.2
  10.9 2.4 collective-permute-start.3
  13.2 1.6 fusion.46
  14.8 4.0 %collective-permute-start = (f32[3,8,1,128]{3,2,1,0:T(1,128)}, f32[3,8,1,128]{3,2,1,0:T(1,128)}, u32[]{:S(2)}, u32[]{:S(2)}) collective-permute-start(f32[3,8,1,128]{3,2,1,0:T(1,128)} %get-tuple-element.94), channel_id=1, source_target_pairs={{0,1},{1,2},{2,3},{3,4},{4,5},{5,6},{6,7},{7,8},{8,9},{9,10},{10,1... | collective-permute-start | bytes 36872 | tf_op jit(solution)/shard_map/ppermute | solution.py:33
  20.1 0.9 fusion.44
  21.0 1.5 convolution_bitcast_fusion
  22.5 1.5 fusion.23
  24.0 1.5 convolution_bitcast_fusion.1
  26.2 0.8 select_reduce_fusion
  27.7 1.2 reshape.297
  32.6 2.1 reshape.300
  35.6 0.9 convolution_convert_fusion.1
  37.3 3.3 all-to-all-start
  41.0 4.7 %all-to-all-done = bf16[8,2,259]{2,1,0:T(2,128)(2,1)S(1)} async-done(((bf16[8,2,259]{2,1,0:T(2,128)(2,1)}), bf16[8,2,259]{2,1,0:T(2,128)(2,1)S(1)}, u32[]{:S(2)}, u32[]{:S(2)}) %all-to-all-start) | async-done | bytes 8320 | tf_op jit(solution)/shard_map/all_to_all | solution.py:50
  46.0 0.9 convolution_multiply_fusion.4
  46.9 4.5 %fusion.14 = (f32[16,4,4,8,64]{4,0,3,2,1:T(8,128)}, f32[16,4,4,8,64]{4,0,3,2,1:T(8,128)}) fusion(bf16[3,3,3,64,64]{4,3,2,1,0:T(8,128)(2,1)} %bitcast.138, f32[16,4,4,8,64]{4,0,3,2,1:T(8,128)S(1)} %convolution_multiply_fusion.4), kind=kOutput, calls=%fused_computation.26 | convolution fusion | flops 289669120 | bytes 1794048 | tf_op jit(solution)/shard_map/conv_general_dilated | solution.py:130
  51.4 1.3 reduce_sum.75
  53.1 4.6 %multiply_convert_fusion.3 = (bf16[16,2048]{1,0:T(8,128)(2,1)S(1)}, f32[16,2048]{1,0:T(8,128)S(1)}) fusion(bf16[16,2048]{1,0:T(8,128)(2,1)S(1)} %convert_element_type.116, bf16[1,2048,2048]{2,1,0:T(8,128)(2,1)} %param.23), kind=kOutput, calls=%fused_computation.50 | convolution fusion | flops 134414336 | bytes 8650752 | tf_op jit(solution)/shard_map/dot_general | solution.py:164
  58.6 5.4 %all-gather = bf16[32,2048]{1,0:T(8,128)(2,1)} all-gather(bf16[16,2048]{1,0:T(8,128)(2,1)S(1)} %fusion.11), channel_id=2, replica_groups=mesh['wall'=8,'stream_0'=8,'stream_1'=2,'stream_2'=2] {'stream_1'}, dimensions={0}, use_global_device_ids=true | all-gather | bytes 196608 | tf_op jit(solution)/shard_map/all_gather | solution.py:64
  66.6 5.7 %fusion.8 = f32[16,2048]{1,0:T(8,128)S(1)} fusion(bf16[16,2048]{1,0:T(8,128)(2,1)S(1)} %fusion.11, bf16[1,2048,2048]{2,1,0:T(8,128)(2,1)} %param.23), kind=kOutput, calls=%fused_computation.9 | convolution fusion | flops 134250496 | bytes 8585216 | tf_op jit(solution)/shard_map/dot_general | solution.py:174
  73.1 3.6 %convolution_multiply_fusion.5 = f32[3,3,3,64,64]{4,3,2,1,0:T(8,128)} fusion(bf16[16,4,4,8,64]{4,0,3,2,1:T(8,128)(2,1)S(1)} %multiply_convert_fusion, f32[16,4,4,8,64]{4,0,3,2,1:T(8,128)S(1)} %convolution_multiply_fusion.4), kind=kOutput, calls=%fused_computation.16 | convolution fusion | flops 289124352 | bytes 1228800 | tf_op jit(solution)/shard_map/transpose | solution.py:144
  77.1 4.2 %convolution_multiply_fusion.6 = f32[3,3,3,2,64]{4,3,2,1,0:T(2,128)S(1)} fusion(bf16[16,2,4,4,8]{0,4,3,2,1:T(8,128)(2,1)S(1)} %bitcast.141, bf16[16,4,4,8,64]{4,0,3,2,1:T(8,128)(2,1)S(1)} %multiply_convert_fusion, bf16[3,3,3,64,64]{4,3,2,1,0:T(8,128)(2,1)S(1)} %bitcast.139, f32[16,4,4,8,64]{4,0,3,2,1:T(8,128)S(1)} %convolution_multiply_fusion.4), kind=kOutput, calls=%fused_computation.20 | convolution fusion | flops 298683776 | bytes 1029632 | tf_op jit(solution)/shard_map/transpose | solution.py:144
  81.3 19.8 %all-gather.6.cloned.1.call-done = bf16[16,16,2048]{2,1,0:T(8,128)(2,1)} async-done(((bf16[2,16,2048]{2,1,0:T(8,128)(2,1)}), bf16[16,16,2048]{2,1,0:T(8,128)(2,1)}) %all-gather.6.cloned.1.call-update) | async-done | bytes 1048592 | tf_op jit(solution)/shard_map/all_gather | solution.py:64
  102.0 4.9 %all-to-all-start.1 = ((f32[8,2,2]{1,2,0:T(2,128)}), f32[8,2,2]{1,2,0:T(2,128)S(1)}, u32[]{:S(2)}, u32[]{:S(2)}) async-start(f32[8,2,2]{1,2,0:T(2,128)} %copy.77), calls=%async_computation.1 | async-start | bytes 16384 | tf_op jit(solution)/shard_map/all_to_all | solution.py:266
  107.0 128.6 %all-reduce = (f32[54,64]{1,0:T(8,128)S(1)}, f32[2048,2]{0,1:T(2,128)S(1)}) all-reduce(f32[54,64]{1,0:T(8,128)S(1)} %reshape.304, f32[2048,2]{0,1:T(2,128)S(1)} %convolution_multiply_fusion.1), channel_id=1, replica_groups=mesh['wall'=8,'stream_0'=8,'stream_1'=2,'stream_2'=2] {'stream_0','strea..., use_global_device_ids=true, to_apply=%region_5.6 | all-reduce | flops 7552 | bytes 60416 | tf_op jit(solution)/shard_map/psum | solution.py:282
  239.1 10.2 %all-to-all-start.2 = ((bf16[32,2,512]{2,1,0:T(2,128)(2,1)}), bf16[32,2,512]{2,1,0:T(2,128)(2,1)S(1)}, u32[]{:S(2)}, u32[]{:S(2)}) async-start(bf16[32,2,512]{2,1,0:T(2,128)(2,1)} %reshape.333), calls=%async_computation.2 | async-start | bytes 131072 | tf_op jit(solution)/shard_map/all_to_all | solution.py:271
  250.2 9.0 %all-to-all-done.2 = bf16[32,2,512]{2,1,0:T(2,128)(2,1)S(1)} async-done(((bf16[32,2,512]{2,1,0:T(2,128)(2,1)}), bf16[32,2,512]{2,1,0:T(2,128)(2,1)S(1)}, u32[]{:S(2)}, u32[]{:S(2)}) %all-to-all-start.2) | async-done | bytes 65568 | tf_op jit(solution)/shard_map/all_to_all | solution.py:271
  259.3 84.0 %all-reduce.3.cloned.1.call-done = f32[27,64,64]{2,1,0:T(8,128)} async-done(((f32[27,64,64]{2,1,0:T(8,128)}), f32[27,64,64]{2,1,0:T(8,128)}) %all-reduce.3.cloned.1.call-update) | async-done | bytes 442384 | tf_op jit(solution)/shard_map/psum | solution.py:282
  343.3 1.5 multiply_reduce_fusion
  344.7 2.4 fusion.15
  347.1 1.7 copy.82
  349.5 1.9 fusion.16
  (120 shorter events, 19.6 us)
Async XLA Ops:
  8.0 32.9 %copy-start = (f32[3,8,16,128]{3,2,1,0:T(8,128)S(1)}, f32[3,8,16,128]{3,2,1,0:T(8,128)}, u32[]{:S(2)}) copy-start(f32[3,8,16,128]{3,2,1,0:T(8,128)} %param.18) | copy-start | bytes 589828
  8.0 32.9 %copy-start.9 = (bf16[1,54,64]{2,1,0:T(8,128)(2,1)S(1)}, bf16[1,54,64]{2,1,0:T(8,128)(2,1)}, u32[]{:S(2)}) copy-start(bf16[1,54,64]{2,1,0:T(8,128)(2,1)} %param.21) | copy-start | bytes 20740
  8.8 22.3 %collective-permute-start.2 = (f32[3,1,16,128]{3,2,1,0:T(8,128)S(1)}, f32[3,1,16,128]{3,2,1,0:T(8,128)S(1)}, u32[]{:S(2)}, u32[]{:S(2)}) collective-permute-start(f32[3,1,16,128]{3,2,1,0:T(8,128)S(1)} %get-tuple-element.96), channel_id=1, source_target_pairs={{0,32},{32,64},{64,96},{96,128},{128,160},{160,192},{192,224},{224... | collective-permute-start | bytes 73736 | tf_op jit(solution)/shard_map/ppermute | solution.py:33
  10.9 20.3 %collective-permute-start.3 = (f32[3,1,16,128]{3,2,1,0:T(8,128)S(1)}, f32[3,1,16,128]{3,2,1,0:T(8,128)S(1)}, u32[]{:S(2)}, u32[]{:S(2)}) collective-permute-start(f32[3,1,16,128]{3,2,1,0:T(8,128)S(1)} %get-tuple-element.95), channel_id=1, source_target_pairs={{32,0},{64,32},{96,64},{128,96},{160,128},{192,160},{224,192},{0,2... | collective-permute-start | bytes 73736 | tf_op jit(solution)/shard_map/ppermute | solution.py:34
  14.8 49.3 %collective-permute-start = (f32[3,8,1,128]{3,2,1,0:T(1,128)}, f32[3,8,1,128]{3,2,1,0:T(1,128)}, u32[]{:S(2)}, u32[]{:S(2)}) collective-permute-start(f32[3,8,1,128]{3,2,1,0:T(1,128)} %get-tuple-element.94), channel_id=1, source_target_pairs={{0,1},{1,2},{2,3},{3,4},{4,5},{5,6},{6,7},{7,8},{8,9},{9,10},{10,1... | collective-permute-start | bytes 36872 | tf_op jit(solution)/shard_map/ppermute | solution.py:33
  18.8 46.1 %collective-permute-start.1 = (f32[3,8,1,128]{3,2,1,0:T(1,128)S(1)}, f32[3,8,1,128]{3,2,1,0:T(1,128)}, u32[]{:S(2)}, u32[]{:S(2)}) collective-permute-start(f32[3,8,1,128]{3,2,1,0:T(1,128)S(1)} %get-tuple-element.93), channel_id=1, source_target_pairs={{1,0},{2,1},{3,2},{4,3},{5,4},{6,5},{7,6},{8,7},{9,8},{10,9},{11,1... | collective-permute-start | bytes 36872 | tf_op jit(solution)/shard_map/ppermute | solution.py:34
  20.1 10.4 %copy-start.18 = (pred[8]{0:T(512)(128)(4,1)}, pred[8]{0:T(512)(128)(4,1)S(1)}, u32[]{:S(2)}) copy-start(pred[8]{0:T(512)(128)(4,1)S(1)} %compare_and_fusion) | copy-start | bytes 28
  27.7 23.7 %copy-start.16 = (s32[8]{0:T(128)}, s32[8]{0:T(128)S(1)}, u32[]{:S(2)}) copy-start(s32[8]{0:T(128)S(1)} %multiply_add_fusion) | copy-start | bytes 100
  31.2 0.7 copy-start.1
  37.3 8.3 %all-to-all-start = ((bf16[8,2,259]{2,1,0:T(2,128)(2,1)}), bf16[8,2,259]{2,1,0:T(2,128)(2,1)S(1)}, u32[]{:S(2)}, u32[]{:S(2)}) async-start(bf16[8,2,259]{2,1,0:T(2,128)(2,1)} %pad_maximum_fusion.2), calls=%async_computation | async-start | bytes 24576 | tf_op jit(solution)/shard_map/all_to_all | solution.py:50
  40.7 60.5 %all-gather.6.cloned.1.call-start = ((), (), s32[]{:S(2)}) async-start(), calls=%async_computation.4 | async-start | bytes 1179648 | tf_op jit(solution)/shard_map/all_gather | solution.py:64
  45.9 12.5 %copy-start.12 = (f32[16]{0:T(128)}, f32[16]{0:T(128)S(1)}, u32[]{:S(2)}) copy-start(f32[16]{0:T(128)S(1)} %convert_reduce_fusion) | copy-start | bytes 196
  46.0 5.4 %copy-start.7 = (bf16[16,256]{0,1:T(8,128)(2,1)}, bf16[16,256]{0,1:T(8,128)(2,1)S(1)}, u32[]{:S(2)}) copy-start(bf16[16,256]{0,1:T(8,128)(2,1)S(1)} %copy.74) | copy-start | bytes 24580
  52.7 5.0 %copy-start.10 = (bf16[1,2048,2]{1,2,0:T(2,128)(2,1)S(1)}, bf16[1,2048,2]{1,2,0:T(2,128)(2,1)}, u32[]{:S(2)}) copy-start(bf16[1,2048,2]{1,2,0:T(2,128)(2,1)} %param.24) | copy-start | bytes 24580
  53.1 5.6 %copy-start.14 = (bf16[16,2]{0,1:T(2,128)(2,1)}, bf16[16,2]{0,1:T(2,128)(2,1)S(1)}, u32[]{:S(2)}) copy-start(bf16[16,2]{0,1:T(2,128)(2,1)S(1)} %copy.88) | copy-start | bytes 196
  53.1 12.7 %copy-start.2 = (f32[3,8,16,128]{3,2,1,0:T(8,128)S(1)}, f32[3,8,16,128]{3,2,1,0:T(8,128)}, u32[]{:S(2)}) copy-start(f32[3,8,16,128]{3,2,1,0:T(8,128)} %copy-done.1) | copy-start | bytes 589828
  57.7 0.6 copy-start.5
  64.1 279.2 %all-reduce.3.cloned.1.call-start = ((), (), s32[]{:S(2)}) async-start(), calls=%async_computation.3 | async-start | bytes 1769472 | tf_op jit(solution)/shard_map/psum | solution.py:282
  66.6 6.1 %copy-start.3 = (f32[16,4,4,8,64]{4,0,3,2,1:T(8,128)S(1)}, f32[16,4,4,8,64]{4,0,3,2,1:T(8,128)}, u32[]{:S(2)}) copy-start(f32[16,4,4,8,64]{4,0,3,2,1:T(8,128)} %get-tuple-element.98) | copy-start | bytes 1572868
  72.7 4.4 %copy-start.4 = (bf16[1,27,64,64]{3,2,1,0:T(8,128)(2,1)S(1)}, bf16[1,27,64,64]{3,2,1,0:T(8,128)(2,1)}, u32[]{:S(2)}) copy-start(bf16[1,27,64,64]{3,2,1,0:T(8,128)(2,1)} %param.22) | copy-start | bytes 663556
  72.7 4.4 %copy-start.8 = (bf16[16,256]{0,1:T(8,128)(2,1)S(1)}, bf16[16,256]{0,1:T(8,128)(2,1)}, u32[]{:S(2)}) copy-start(bf16[16,256]{0,1:T(8,128)(2,1)} %copy-done.7) | copy-start | bytes 24580
  76.8 24.4 %copy-start.6 = (bf16[16,2048]{1,0:T(8,128)(2,1)S(1)}, bf16[16,2048]{1,0:T(8,128)(2,1)}, u32[]{:S(2)}) copy-start(bf16[16,2048]{1,0:T(8,128)(2,1)} %copy-done.5) | copy-start | bytes 196612
  76.8 24.4 %copy-start.13 = (f32[16]{0:T(128)S(1)}, f32[16]{0:T(128)}, u32[]{:S(2)}) copy-start(f32[16]{0:T(128)} %copy-done.12) | copy-start | bytes 196
  76.8 24.4 %copy-start.15 = (bf16[16,2]{0,1:T(2,128)(2,1)S(1)}, bf16[16,2]{0,1:T(2,128)(2,1)}, u32[]{:S(2)}) copy-start(bf16[16,2]{0,1:T(2,128)(2,1)} %copy-done.14) | copy-start | bytes 196
  76.8 160.9 %copy-start.11 = (bf16[1,2048,2]{1,2,0:T(2,128)(2,1)S(1)}, bf16[1,2048,2]{1,2,0:T(2,128)(2,1)}, u32[]{:S(2)}) copy-start(bf16[1,2048,2]{1,2,0:T(2,128)(2,1)} %param.24) | copy-start | bytes 24580
  76.8 172.6 %copy-start.17 = (s32[8]{0:T(128)S(1)}, s32[8]{0:T(128)}, u32[]{:S(2)}) copy-start(s32[8]{0:T(128)} %copy-done.16) | copy-start | bytes 100
  76.8 270.3 %all-gather.8.cloned.1.call-start = ((), (), s32[]{:S(2)}) async-start(), calls=%async_computation.5 | async-start | bytes 3145728 | tf_op jit(solution)/shard_map/all_gather | solution.py:64
  102.0 137.1 %all-to-all-start.1 = ((f32[8,2,2]{1,2,0:T(2,128)}), f32[8,2,2]{1,2,0:T(2,128)S(1)}, u32[]{:S(2)}, u32[]{:S(2)}) async-start(f32[8,2,2]{1,2,0:T(2,128)} %copy.77), calls=%async_computation.1 | async-start | bytes 16384 | tf_op jit(solution)/shard_map/all_to_all | solution.py:266
  239.1 20.0 %all-to-all-start.2 = ((bf16[32,2,512]{2,1,0:T(2,128)(2,1)}), bf16[32,2,512]{2,1,0:T(2,128)(2,1)S(1)}, u32[]{:S(2)}, u32[]{:S(2)}) async-start(bf16[32,2,512]{2,1,0:T(2,128)(2,1)} %reshape.333), calls=%async_computation.2 | async-start | bytes 131072 | tf_op jit(solution)/shard_map/all_to_all | solution.py:271
Sparse Core Ops, SparseCore 0:
  64.2 36.9 all-gather.5
  103.1 19.9 all-gather.7
Sparse Core Ops, SparseCore 1:
  76.8 266.4 all-reduce.2
where the time goes:
time: 360 us; the launch traced here: 359 us
  blocking collectives  134 us (37%)
  waiting for transfers between devices  117 us (32%)
  matrix products  31 us (9%)
  starting transfers between devices  27.4 us (8%)
  between operations  16.8 us (5%)
  other arithmetic  16.6 us (5%)
  local copies, waits for them, and re-layouts  15.5 us (4%)
    psum x1, blocking collectives, body(): lax.psum((grad_one, grad_two, grad_out), STREAM)  129 us
    psum x1, waiting for transfers between devices, body(): lax.psum((grad_one, grad_two, grad_out), STREAM)  84 us
    all_gather x2, waiting for transfers between devices, gather_in_order(): tiles = lax.all_gather(tiles, axes[k])  19.8 us
    all_to_all x1, starting transfers between devices, body(): lax.all_to_all(features, STREAM, split_axis=1, concat_axis=0, tiled=True)  10.2 us
    all_to_all x1, waiting for transfers between devices, body(): lax.all_to_all(features, STREAM, split_axis=1, concat_axis=0, tiled=True)  8.98 us
    transpose x2, matrix products, conv_filter(): return jnp.moveaxis(taps, 0, 3)  7.83 us
  transfers between devices with their start and end apart: 10, of which 4 were waited for; matrix products, arithmetic and copies ran while one was open for 16% of the time, Pallas kernels for 0%

commit v1 on v0

--- a/solution.py
+++ b/solution.py
@@ -5,6 +5,7 @@
 from jax import lax
 from jax.sharding import Mesh
 from jax.sharding import PartitionSpec as P
+from jax.lax import psum
 
 P_SIZE = 8
 PY = 4
@@ -279,7 +280,9 @@
     )
     own_rows = lax.dynamic_slice_in_dim(w_hidden[0], flow_place * share_rows, share_rows, 0)
     new_w_hidden = row_update(own_rows, grad_hidden)[None]
-    grad_one, grad_two, grad_out = lax.psum((grad_one, grad_two, grad_out), STREAM)
+    grad_one, grad_two, grad_out = psum(
+        psum((grad_one, grad_two, grad_out), ("stream_1", "stream_2")), axis_name="stream_0"
+    )
     new_k_second = row_update(k_second[0], grad_two)
     new_k_first = row_update(k_first[0], grad_one)
     new_w_out = whole_update(w_out[0], grad_out)

time: 360 us -> 213 us (0.59)
  blocking collectives: 134 us -> 42.9 us
  waiting for transfers between devices: 117 us -> 58.6 us
  starting transfers between devices: 27.4 us -> 32.9 us
    psum x1 -> x2, blocking collectives: 129 us -> 37.5 us  [the longest x1 23.9 us: body(): psum(psum((grad_one, grad_two, grad_out), ('stream_1', 'stream_2')), axis...]
    psum x1 -> x2, waiting for transfers between devices: 84 us -> 31.5 us  [the longest x1 31.4 us: body(): psum((grad_one, grad_two, grad_out), ('stream_1', 'stream_2'))]
    all_gather x2, waiting for transfers between devices: 19.8 us -> 11.7 us  [gather_in_order(): tiles = lax.all_gather(tiles, axes[k])]
    all_to_all x1, starting transfers between devices: 10.2 us -> 14.2 us  [body(): lax.all_to_all(features, STREAM, split_axis=1, concat_axis=0, tiled=True)]
  transfers between devices with their start and end apart: 10 -> 11, of which waited for: 4 -> 5; matrix products, arithmetic and copies ran while one was open for 16% -> 15% of each run, Pallas kernels for 0% -> 0%
where the time goes in v1:
time: 213 us; the launch traced here: 212 us
  waiting for transfers between devices  58.6 us (28%)
  blocking collectives  42.9 us (20%)
  starting transfers between devices  32.9 us (15%)
  matrix products  28.1 us (13%)
  other arithmetic  17.4 us (8%)
  between operations  17 us (8%)
  local copies, waits for them, and re-layouts  15.5 us (7%)
    psum x1, waiting for transfers between devices, body(): psum((grad_one, grad_two, grad_out), ('stream_1', 'stream_2'))  31.4 us
    psum x1, blocking collectives, body(): psum(psum((grad_one, grad_two, grad_out), ('stream_1', 'stream_2')), axis...  23.9 us
    all_to_all x1, starting transfers between devices, body(): lax.all_to_all(features, STREAM, split_axis=1, concat_axis=0, tiled=True)  14.2 us
    psum x1, blocking collectives, body(): psum((grad_one, grad_two, grad_out), ('stream_1', 'stream_2'))  13.6 us
    all_gather x2, waiting for transfers between devices, gather_in_order(): tiles = lax.all_gather(tiles, axes[k])  11.7 us
    all_to_all x1, waiting for transfers between devices, body(): lax.all_to_all(features, STREAM, split_axis=1, concat_axis=0, tiled=True)  9.19 us
    transpose x2, matrix products, conv_filter(): return jnp.moveaxis(taps, 0, 3)  8.93 us
    ppermute x2, starting transfers between devices, extended(): lax.ppermute(last, axis, up)  8.42 us
  transfers between devices with their start and end apart: 11, of which 5 were waited for; matrix products, arithmetic and copies ran while one was open for 15% of the time, Pallas kernels for 0%

profile of v1, /device:TPU:1, one launch (start us, length us, event | category | flops | bytes accessed | tf_op | source)
XLA Modules:
  0.0 212.4 jit_solution(17892379009188051974)
XLA Ops:
  8.8 2.0 collective-permute-start.2
  10.9 2.3 %collective-permute-start.3 = (f32[3,1,16,128]{3,2,1,0:T(8,128)S(1)}, f32[3,1,16,128]{3,2,1,0:T(8,128)S(1)}, u32[]{:S(2)}, u32[]{:S(2)}) collective-permute-start(f32[3,1,16,128]{3,2,1,0:T(8,128)S(1)} %get-tuple-element.97), channel_id=1, source_target_pairs={{32,0},{64,32},{96,64},{128,96},{160,128},{192,160},{224,192},{0,2... | collective-permute-start | bytes 73736 | tf_op jit(solution)/shard_map/ppermute | solution.py:35
  14.5 0.9 fusion.44
  15.4 1.5 fusion.23
  17.7 0.8 select_reduce_fusion
  19.2 1.2 reshape.297
  22.7 1.1 reshape.300
  25.8 3.3 %all-to-all-start = ((bf16[8,2,259]{2,1,0:T(2,128)(2,1)}), bf16[8,2,259]{2,1,0:T(2,128)(2,1)S(1)}, u32[]{:S(2)}, u32[]{:S(2)}) async-start(bf16[8,2,259]{2,1,0:T(2,128)(2,1)} %pad_maximum_fusion.2), calls=%async_computation | async-start | bytes 24576 | tf_op jit(solution)/shard_map/all_to_all | solution.py:51
  29.4 4.7 %all-to-all-done = bf16[8,2,259]{2,1,0:T(2,128)(2,1)S(1)} async-done(((bf16[8,2,259]{2,1,0:T(2,128)(2,1)}), bf16[8,2,259]{2,1,0:T(2,128)(2,1)S(1)}, u32[]{:S(2)}, u32[]{:S(2)}) %all-to-all-start) | async-done | bytes 8320 | tf_op jit(solution)/shard_map/all_to_all | solution.py:51
  35.6 0.9 convolution_multiply_fusion.4
  36.6 3.1 %fusion.14 = (f32[16,4,4,8,64]{4,0,3,2,1:T(8,128)S(1)}, f32[16,4,4,8,64]{4,0,3,2,1:T(8,128)}) fusion(bf16[3,3,3,64,64]{4,3,2,1,0:T(8,128)(2,1)S(1)} %bitcast.139, f32[16,4,4,8,64]{4,0,3,2,1:T(8,128)S(1)} %convolution_multiply_fusion.4), kind=kOutput, calls=%fused_computation.26 | convolution fusion | flops 289669120 | bytes 1794048 | tf_op jit(solution)/shard_map/conv_general_dilated | solution.py:131
  40.1 4.6 %multiply_convert_fusion.3 = (bf16[16,2048]{1,0:T(8,128)(2,1)S(1)}, f32[16,2048]{1,0:T(8,128)S(1)}) fusion(bf16[16,2048]{1,0:T(8,128)(2,1)S(1)} %convert_element_type.116, bf16[1,2048,2048]{2,1,0:T(8,128)(2,1)} %param.23), kind=kOutput, calls=%fused_computation.50 | convolution fusion | flops 134414336 | bytes 8650752 | tf_op jit(solution)/shard_map/dot_general | solution.py:165
  45.7 5.7 %fusion.8 = f32[16,2048]{1,0:T(8,128)S(1)} fusion(bf16[16,2048]{1,0:T(8,128)(2,1)S(1)} %fusion.11, bf16[1,2048,2048]{2,1,0:T(8,128)(2,1)} %param.23), kind=kOutput, calls=%fused_computation.9 | convolution fusion | flops 134250496 | bytes 8585216 | tf_op jit(solution)/shard_map/dot_general | solution.py:175
  52.2 3.6 %convolution_multiply_fusion.5 = f32[3,3,3,64,64]{4,3,2,1,0:T(8,128)} fusion(bf16[16,4,4,8,64]{4,0,3,2,1:T(8,128)(2,1)S(1)} %multiply_convert_fusion, f32[16,4,4,8,64]{4,0,3,2,1:T(8,128)S(1)} %convolution_multiply_fusion.4), kind=kOutput, calls=%fused_computation.16 | convolution fusion | flops 289124352 | bytes 1228800 | tf_op jit(solution)/shard_map/transpose | solution.py:145
  55.9 5.4 %all-gather = bf16[32,2048]{1,0:T(8,128)(2,1)} all-gather(bf16[16,2048]{1,0:T(8,128)(2,1)S(1)} %copy-done.5), channel_id=2, replica_groups=mesh['wall'=8,'stream_0'=8,'stream_1'=2,'stream_2'=2] {'stream_1'}, dimensions={0}, use_global_device_ids=true | all-gather | bytes 196608 | tf_op jit(solution)/shard_map/all_gather | solution.py:65
  62.0 6.4 %collective-permute-start = (f32[3,8,1,128]{3,2,1,0:T(1,128)}, f32[3,8,1,128]{3,2,1,0:T(1,128)}, u32[]{:S(2)}, u32[]{:S(2)}) collective-permute-start(f32[3,8,1,128]{3,2,1,0:T(1,128)} %get-tuple-element.96), channel_id=1, source_target_pairs={{0,1},{1,2},{2,3},{3,4},{4,5},{5,6},{6,7},{7,8},{8,9},{9,10},{10,1... | collective-permute-start | bytes 36872 | tf_op jit(solution)/shard_map/ppermute | solution.py:34
  70.1 1.3 slice_add_fusion.5
  72.2 1.5 collective-permute-done.1
  73.6 1.3 slice_add_fusion.4
  75.7 1.7 fusion.20
  77.4 31.4 %all-reduce.5.cloned.1.call-done = f32[27,64,64]{2,1,0:T(8,128)} async-done(((f32[27,64,64]{2,1,0:T(8,128)}), f32[27,64,64]{2,1,0:T(8,128)}) %all-reduce.5.cloned.1.call-update) | async-done | bytes 442384 | tf_op jit(solution)/shard_map/psum | solution.py:284
  108.9 5.3 %convolution_multiply_fusion.6 = f32[3,3,3,2,64]{4,3,2,1,0:T(2,128)S(1)} fusion(bf16[16,2,4,4,8]{0,4,3,2,1:T(8,128)(2,1)} %bitcast.141, bf16[16,4,4,8,64]{4,0,3,2,1:T(8,128)(2,1)S(1)} %multiply_convert_fusion, bf16[3,3,3,64,64]{4,3,2,1,0:T(8,128)(2,1)} %bitcast.138, f32[16,4,4,8,64]{4,0,3,2,1:T(8,128)S(1)} %convolution_multiply_fusion.4), kind=kOutput, calls=%fused_computation.20 | convolution fusion | flops 298683776 | bytes 1029632 | tf_op jit(solution)/shard_map/transpose | solution.py:145
  115.2 4.2 %all-to-all-start.1 = ((f32[8,2,2]{1,2,0:T(2,128)}), f32[8,2,2]{1,2,0:T(2,128)S(1)}, u32[]{:S(2)}, u32[]{:S(2)}) async-start(f32[8,2,2]{1,2,0:T(2,128)} %copy.77), calls=%async_computation.1 | async-start | bytes 16384 | tf_op jit(solution)/shard_map/all_to_all | solution.py:267
  119.4 13.6 %all-reduce.1 = (f32[54,64]{1,0:T(8,128)S(1)}, f32[2048,2]{0,1:T(2,128)S(1)}) all-reduce(f32[54,64]{1,0:T(8,128)S(1)} %reshape.304, f32[2048,2]{0,1:T(2,128)S(1)} %convolution_multiply_fusion.1), channel_id=1, replica_groups=mesh['wall'=8,'stream_0'=8,'stream_1'=2,'stream_2'=2] {'stream_1','strea..., use_global_device_ids=true, to_apply=%region_5.6 | all-reduce | flops 7552 | bytes 60416 | tf_op jit(solution)/shard_map/psum | solution.py:284
  133.0 23.9 %all-reduce = (f32[54,64]{1,0:T(8,128)S(1)}, f32[2048,2]{0,1:T(2,128)S(1)}) all-reduce(f32[54,64]{1,0:T(8,128)S(1)} %get-tuple-element.86, f32[2048,2]{0,1:T(2,128)S(1)} %get-tuple-element.87), channel_id=1, replica_groups=mesh['wall'=8,'stream_0'=8,'stream_1'=2,'stream_2'=2] {'stream_0'}, use_global_device_ids=true, to_apply=%region_6.7 | all-reduce | flops 7552 | bytes 60416 | tf_op jit(solution)/shard_map/psum | solution.py:283
  160.5 14.2 %all-to-all-start.2 = ((bf16[32,2,512]{2,1,0:T(2,128)(2,1)}), bf16[32,2,512]{2,1,0:T(2,128)(2,1)S(1)}, u32[]{:S(2)}, u32[]{:S(2)}) async-start(bf16[32,2,512]{2,1,0:T(2,128)(2,1)} %reshape.333), calls=%async_computation.2 | async-start | bytes 131072 | tf_op jit(solution)/shard_map/all_to_all | solution.py:272
  175.6 9.2 %all-to-all-done.2 = bf16[32,2,512]{2,1,0:T(2,128)(2,1)S(1)} async-done(((bf16[32,2,512]{2,1,0:T(2,128)(2,1)}), bf16[32,2,512]{2,1,0:T(2,128)(2,1)S(1)}, u32[]{:S(2)}, u32[]{:S(2)}) %all-to-all-start.2) | async-done | bytes 65568 | tf_op jit(solution)/shard_map/all_to_all | solution.py:272
  185.0 1.5 multiply_reduce_fusion
  186.5 2.4 %fusion.15 = f32[1,27,64,64]{3,2,1,0:T(8,128)} fusion(f32[27,64,64]{2,1,0:T(8,128)} %all-reduce.7.cloned.1.call-done, bf16[1,27,64,64]{3,2,1,0:T(8,128)(2,1)S(1)} %copy-done.3, f32[27,64]{1,0:T(8,128)S(1)} %add_sqrt_fusion), kind=kLoop, calls=%fused_computation.30 | loop fusion | flops 442368 | bytes 1112832 | tf_op jit(solution)/shard_map/broadcast_in_dim | solution.py:289
  188.8 11.7 %all-gather.8.cloned.1.call-done = bf16[16,2,16,2048]{3,2,1,0:T(8,128)(2,1)} async-done(((bf16[8,2,16,2048]{3,2,1,0:T(8,128)(2,1)}), bf16[16,2,16,2048]{3,2,1,0:T(8,128)(2,1)}) %all-gather.8.cloned.1.call-update) | async-done | bytes 2097168 | tf_op jit(solution)/shard_map/all_gather | solution.py:65
  200.5 1.7 copy.82
  202.9 1.9 fusion.16
  (132 shorter events, 21.0 us)
Async XLA Ops:
  8.0 21.4 %copy-start.10 = (bf16[1,54,64]{2,1,0:T(8,128)(2,1)S(1)}, bf16[1,54,64]{2,1,0:T(8,128)(2,1)}, u32[]{:S(2)}) copy-start(bf16[1,54,64]{2,1,0:T(8,128)(2,1)} %param.21) | copy-start | bytes 20740
  8.0 28.5 %copy-start.2 = (bf16[1,27,64,64]{3,2,1,0:T(8,128)(2,1)S(1)}, bf16[1,27,64,64]{3,2,1,0:T(8,128)(2,1)}, u32[]{:S(2)}) copy-start(bf16[1,27,64,64]{3,2,1,0:T(8,128)(2,1)} %param.22) | copy-start | bytes 663556
  8.8 13.8 %collective-permute-start.2 = (f32[3,1,16,128]{3,2,1,0:T(8,128)S(1)}, f32[3,1,16,128]{3,2,1,0:T(8,128)S(1)}, u32[]{:S(2)}, u32[]{:S(2)}) collective-permute-start(f32[3,1,16,128]{3,2,1,0:T(8,128)S(1)} %get-tuple-element.98), channel_id=1, source_target_pairs={{0,32},{32,64},{64,96},{96,128},{128,160},{160,192},{192,224},{224... | collective-permute-start | bytes 73736 | tf_op jit(solution)/shard_map/ppermute | solution.py:34
  10.9 11.8 %collective-permute-start.3 = (f32[3,1,16,128]{3,2,1,0:T(8,128)S(1)}, f32[3,1,16,128]{3,2,1,0:T(8,128)S(1)}, u32[]{:S(2)}, u32[]{:S(2)}) collective-permute-start(f32[3,1,16,128]{3,2,1,0:T(8,128)S(1)} %get-tuple-element.97), channel_id=1, source_target_pairs={{32,0},{64,32},{96,64},{128,96},{160,128},{192,160},{224,192},{0,2... | collective-permute-start | bytes 73736 | tf_op jit(solution)/shard_map/ppermute | solution.py:35
  19.2 17.4 %copy-start.21 = (s32[8]{0:T(128)}, s32[8]{0:T(128)S(1)}, u32[]{:S(2)}) copy-start(s32[8]{0:T(128)S(1)} %multiply_add_fusion) | copy-start | bytes 100
  25.8 8.3 %all-to-all-start = ((bf16[8,2,259]{2,1,0:T(2,128)(2,1)}), bf16[8,2,259]{2,1,0:T(2,128)(2,1)S(1)}, u32[]{:S(2)}, u32[]{:S(2)}) async-start(bf16[8,2,259]{2,1,0:T(2,128)(2,1)} %pad_maximum_fusion.2), calls=%async_computation | async-start | bytes 24576 | tf_op jit(solution)/shard_map/all_to_all | solution.py:51
  29.2 79.6 %all-reduce.5.cloned.1.call-start = ((), (), s32[]{:S(2)}) async-start(), calls=%async_computation.3 | async-start | bytes 1769472 | tf_op jit(solution)/shard_map/psum | solution.py:284
  35.6 4.0 %copy-start.8 = (bf16[16,256]{0,1:T(8,128)(2,1)}, bf16[16,256]{0,1:T(8,128)(2,1)S(1)}, u32[]{:S(2)}) copy-start(bf16[16,256]{0,1:T(8,128)(2,1)S(1)} %copy.74) | copy-start | bytes 24580
  39.8 5.0 %copy-start.13 = (bf16[1,2048,2]{1,2,0:T(2,128)(2,1)S(1)}, bf16[1,2048,2]{1,2,0:T(2,128)(2,1)}, u32[]{:S(2)}) copy-start(bf16[1,2048,2]{1,2,0:T(2,128)(2,1)} %param.24) | copy-start | bytes 24580
  39.8 5.6 %copy-start.17 = (f32[16]{0:T(128)S(1)}, f32[16]{0:T(128)}, u32[]{:S(2)}) copy-start(f32[16]{0:T(128)} %convert_reduce_fusion) | copy-start | bytes 196
  40.1 5.5 %copy-start.19 = (bf16[16,2]{0,1:T(2,128)(2,1)}, bf16[16,2]{0,1:T(2,128)(2,1)S(1)}, u32[]{:S(2)}) copy-start(bf16[16,2]{0,1:T(2,128)(2,1)S(1)} %copy.88) | copy-start | bytes 196
  44.8 7.0 %copy-start.1 = (f32[16,4,4,8,64]{4,0,3,2,1:T(8,128)S(1)}, f32[16,4,4,8,64]{4,0,3,2,1:T(8,128)}, u32[]{:S(2)}) copy-start(f32[16,4,4,8,64]{4,0,3,2,1:T(8,128)} %get-tuple-element.100) | copy-start | bytes 1572868
  44.9 6.8 %copy-start.15 = (f32[16,2]{0,1:T(2,128)}, f32[16,2]{0,1:T(2,128)S(1)}, u32[]{:S(2)}) copy-start(f32[16,2]{0,1:T(2,128)S(1)} %convolution_multiply_fusion.7) | copy-start | bytes 388
  45.6 6.1 %copy-start.4 = (bf16[16,2048]{1,0:T(8,128)(2,1)}, bf16[16,2048]{1,0:T(8,128)(2,1)S(1)}, u32[]{:S(2)}) copy-start(bf16[16,2048]{1,0:T(8,128)(2,1)S(1)} %fusion.11) | copy-start | bytes 196612
  51.7 9.6 %copy-start = (f32[3,8,16,128]{3,2,1,0:T(8,128)S(1)}, f32[3,8,16,128]{3,2,1,0:T(8,128)}, u32[]{:S(2)}) copy-start(f32[3,8,16,128]{3,2,1,0:T(8,128)} %param.18) | copy-start | bytes 589828
  52.2 3.7 %copy-start.5 = (bf16[16,2048]{1,0:T(8,128)(2,1)S(1)}, bf16[16,2048]{1,0:T(8,128)(2,1)}, u32[]{:S(2)}) copy-start(bf16[16,2048]{1,0:T(8,128)(2,1)} %copy-done.4) | copy-start | bytes 196612
  52.2 16.2 %copy-start.12 = (f32[32,16,1,1]{0,1,3,2:T(8,128)S(1)}, f32[32,16,1,1]{0,1,3,2:T(8,128)}, u32[]{:S(2)}) copy-start(f32[32,16,1,1]{0,1,3,2:T(8,128)} %constant.248) | copy-start | bytes 6148
  52.2 16.7 %copy-start.9 = (f32[256,128,1,1]{1,0,3,2:T(8,128)S(1)}, f32[256,128,1,1]{1,0,3,2:T(8,128)}, u32[]{:S(2)}) copy-start(f32[256,128,1,1]{1,0,3,2:T(8,128)} %constant.250) | copy-start | bytes 393220
  55.8 58.5 %all-gather.6.cloned.1.call-start = ((), (), s32[]{:S(2)}) async-start(), calls=%async_computation.5 | async-start | bytes 1179648 | tf_op jit(solution)/shard_map/all_gather | solution.py:65
  61.3 123.6 %all-reduce.7.cloned.1.call-start = ((), (), s32[]{:S(2)}) async-start(), calls=%async_computation.4 | async-start | bytes 1769472 | tf_op jit(solution)/shard_map/psum | solution.py:283
  62.0 8.1 %collective-permute-start = (f32[3,8,1,128]{3,2,1,0:T(1,128)}, f32[3,8,1,128]{3,2,1,0:T(1,128)}, u32[]{:S(2)}, u32[]{:S(2)}) collective-permute-start(f32[3,8,1,128]{3,2,1,0:T(1,128)} %get-tuple-element.96), channel_id=1, source_target_pairs={{0,1},{1,2},{2,3},{3,4},{4,5},{5,6},{6,7},{7,8},{8,9},{9,10},{10,1... | collective-permute-start | bytes 36872 | tf_op jit(solution)/shard_map/ppermute | solution.py:34
  68.4 5.2 %collective-permute-start.1 = (f32[3,8,1,128]{3,2,1,0:T(1,128)}, f32[3,8,1,128]{3,2,1,0:T(1,128)}, u32[]{:S(2)}, u32[]{:S(2)}) collective-permute-start(f32[3,8,1,128]{3,2,1,0:T(1,128)} %get-tuple-element.95), channel_id=1, source_target_pairs={{1,0},{2,1},{3,2},{4,3},{5,4},{6,5},{7,6},{8,7},{9,8},{10,9},{11,1... | collective-permute-start | bytes 36872 | tf_op jit(solution)/shard_map/ppermute | solution.py:35
  108.8 5.5 %copy-start.7 = (bf16[16,2048]{1,0:T(8,128)(2,1)S(1)}, bf16[16,2048]{1,0:T(8,128)(2,1)}, u32[]{:S(2)}) copy-start(bf16[16,2048]{1,0:T(8,128)(2,1)} %copy-done.6) | copy-start | bytes 196612
  108.8 5.5 %copy-start.16 = (f32[16,2]{0,1:T(2,128)S(1)}, f32[16,2]{0,1:T(2,128)}, u32[]{:S(2)}) copy-start(f32[16,2]{0,1:T(2,128)} %copy-done.15) | copy-start | bytes 388
  108.8 5.5 %copy-start.18 = (f32[16]{0:T(128)S(1)}, f32[16]{0:T(128)}, u32[]{:S(2)}) copy-start(f32[16]{0:T(128)} %convert_reduce_fusion) | copy-start | bytes 196
  108.9 5.5 %copy-start.20 = (bf16[16,2]{0,1:T(2,128)(2,1)S(1)}, bf16[16,2]{0,1:T(2,128)(2,1)}, u32[]{:S(2)}) copy-start(bf16[16,2]{0,1:T(2,128)(2,1)} %copy-done.19) | copy-start | bytes 196
  108.9 50.3 %copy-start.14 = (bf16[1,2048,2]{1,2,0:T(2,128)(2,1)S(1)}, bf16[1,2048,2]{1,2,0:T(2,128)(2,1)}, u32[]{:S(2)}) copy-start(bf16[1,2048,2]{1,2,0:T(2,128)(2,1)} %param.24) | copy-start | bytes 24580
  108.9 66.0 %copy-start.22 = (s32[8]{0:T(128)S(1)}, s32[8]{0:T(128)}, u32[]{:S(2)}) copy-start(s32[8]{0:T(128)} %copy-done.21) | copy-start | bytes 100
  108.9 77.6 %copy-start.3 = (bf16[1,27,64,64]{3,2,1,0:T(8,128)(2,1)S(1)}, bf16[1,27,64,64]{3,2,1,0:T(8,128)(2,1)}, u32[]{:S(2)}) copy-start(bf16[1,27,64,64]{3,2,1,0:T(8,128)(2,1)} %param.22) | copy-start | bytes 663556
  108.9 91.6 %all-gather.8.cloned.1.call-start = ((), (), s32[]{:S(2)}) async-start(), calls=%async_computation.6 | async-start | bytes 3145728 | tf_op jit(solution)/shard_map/all_gather | solution.py:65
  115.2 45.3 %all-to-all-start.1 = ((f32[8,2,2]{1,2,0:T(2,128)}), f32[8,2,2]{1,2,0:T(2,128)S(1)}, u32[]{:S(2)}, u32[]{:S(2)}) async-start(f32[8,2,2]{1,2,0:T(2,128)} %copy.77), calls=%async_computation.1 | async-start | bytes 16384 | tf_op jit(solution)/shard_map/all_to_all | solution.py:267
  160.5 24.3 %all-to-all-start.2 = ((bf16[32,2,512]{2,1,0:T(2,128)(2,1)}), bf16[32,2,512]{2,1,0:T(2,128)(2,1)S(1)}, u32[]{:S(2)}, u32[]{:S(2)}) async-start(bf16[32,2,512]{2,1,0:T(2,128)(2,1)} %reshape.333), calls=%async_computation.2 | async-start | bytes 131072 | tf_op jit(solution)/shard_map/all_to_all | solution.py:272
  (2 other events, 4.1 us)
Sparse Core Ops, SparseCore 0:
  56.0 52.7 all-reduce.4
Sparse Core Ops, SparseCore 1:
  61.4 38.4 all-gather.5
  108.9 70.1 all-reduce.6
  180.8 19.7 all-gather.7
